TPU v7x, 256 devices: a whole 4x4x8 slice. The times are simulated.
256 devices in a mesh: px: 32 (over z, x_hi, core), py: 8 (over y, x_lo).
Axes of the slice: x: 4 (x_hi: 2, x_lo: 2; x = x_hi * 2 + x_lo), y: 4, z: 8, core: 2. Of those that a mesh axis runs over, the one named last changes fastest.
Arguments:
- table: float32 [25, 50, 1000], replicated, may hold values from -1 to 1
- charge: float32 [128, 32, 8], P('px', 'py'), may hold values from 0.1 to 1
- hit_bins: int32 [128, 32, 8], P('px', 'py'), may hold values from 0 to 49
- hit_ticks: int32 [128, 32, 8], P('px', 'py'), may hold values from 0 to 23
- active: int32 [128, 32], P('px', 'py'), may hold values 0 or 1
- measured: bfloat16 [128, 32, 1024], P('px', 'py'), may hold values from -6 to 6
- row_module: int32 [128], replicated, may hold values from 0 to 6, as said below
- col_module: int32 [32], replicated, may hold values from 0 to 4, as said below
Outputs:
- current: bfloat16 [128, 32, 1024], P('px', 'py')
- table_grad: float32 [25, 50, 1000], P(None, None, 'py')
Inputs may be any that keep to these rules, and one draw needn't show every extreme that they name: `row_module`: starts at 0 and never falls; it rises by one at 6 rows. `col_module`: starts at 0 and never falls; it rises by one at 4 columns.
All inputs are finite; a program needn't handle non-finite values. No bound on the sum of `active` on one device may be relied on, other than what follows from the above.
Results may differ from a plain program's by a relative error of at most 0.014.
Values may be sent and summed in bfloat16 or wider, within the bound.
No kernel may reach another device: no remote copies, remote signals or barrier semaphores. Data moves between devices by JAX's collectives and lax.ppermute only.
A program may use at most 128 MiB of HBM per device.

v0:
```python
import jax
import jax.numpy as jnp
from jax import lax
from jax.sharding import PartitionSpec as P

BINS = 50
SHIFTS = 24


def passed_along(block, axis, distance):
    devices = range(lax.axis_size(axis))
    route = [(i - distance, i) for i in devices if i - distance in devices]
    return lax.ppermute(block, axis, route)


def bin_charges(charge, hit_bins, hit_ticks):
    tick_hot = (hit_ticks[..., None] == jnp.arange(SHIFTS, dtype=jnp.int32)).astype(jnp.float32)
    bin_hot = (hit_bins[..., None] == jnp.arange(BINS, dtype=jnp.int32)).astype(jnp.float32)
    weighted = charge[..., None] * tick_hot
    return jnp.einsum("xyks,xykb->xysb", weighted, bin_hot).astype(jnp.bfloat16)


def gather_offsets(source, rows, cols, count_x, count_y):
    pieces = []
    for row_off in range(-2, 3):
        for col_off in range(-2, 3):
            partial_value = source[
                2 - row_off : 2 - row_off + count_x, 2 - col_off : 2 - col_off + count_y
            ]
            row_same = rows[2 - row_off : 2 - row_off + count_x] == rows[2 : 2 + count_x]
            col_same = cols[2 - col_off : 2 - col_off + count_y] == cols[2 : 2 + count_y]
            allowed = row_same[:, None] & col_same[None, :]
            pieces.append(
                jnp.where(
                    allowed[:, :, None, None], partial_value, jnp.zeros((), partial_value.dtype)
                )
            )
    return jnp.stack(pieces, 0)


def shift_sum(partial_value, ticks):
    total = jnp.zeros(partial_value.shape[:2] + (ticks + SHIFTS,), jnp.float32)
    for offset in range(SHIFTS):
        total = total + jnp.pad(
            partial_value[:, :, offset, :], ((0, 0), (0, 0), (offset, SHIFTS - offset))
        )
    return total


def windows(resid, ticks):
    return jnp.stack([resid[:, :, offset : offset + ticks] for offset in range(SHIFTS)], axis=2)


def residual_of(prediction, measured, active):
    return (
        (prediction - measured.astype(jnp.float32)) * active.astype(jnp.float32)[..., None]
    ).astype(jnp.bfloat16)


def on_device(table, charge, hit_bins, hit_ticks, active, measured, row_module, col_module):
    tile_x, tile_y = (charge.shape[0], charge.shape[1])
    ticks = table.shape[2]
    parts_y = lax.axis_size("py")
    share = ticks // parts_y
    span = share + SHIFTS - 1
    weights = table.astype(jnp.bfloat16)
    row_start = lax.axis_index("px") * tile_x
    col_start = lax.axis_index("py") * tile_y
    deposits = jnp.stack(
        [charge, hit_bins.astype(jnp.float32), hit_ticks.astype(jnp.float32)], axis=-1
    )
    band = lax.all_gather(deposits, "py", axis=1, tiled=True)
    above = passed_along(band[tile_x - 2 :], "px", 1)
    below = passed_along(band[:2], "px", -1)
    wide = jnp.concatenate([above, band, below], axis=0)
    binned = bin_charges(
        wide[..., 0], wide[..., 1].astype(jnp.int32), wide[..., 2].astype(jnp.int32)
    )
    source = jnp.pad(binned, ((0, 0), (2, 2), (0, 0), (0, 0)))
    width = source.shape[1] - 4
    rows_wide = lax.dynamic_slice_in_dim(
        jnp.pad(row_module, 2, constant_values=-1), row_start, tile_x + 4, 0
    )
    cols_all = jnp.pad(col_module, 2, constant_values=-1)
    own_source = lax.dynamic_slice_in_dim(source, col_start, tile_y + 4, 1)
    own_cols = lax.dynamic_slice_in_dim(cols_all, col_start, tile_y + 4, 0)
    stacked = gather_offsets(own_source, rows_wide, own_cols, tile_x, tile_y)
    partial_value = jnp.einsum(
        "oxysb,obt->xyst", stacked, weights, preferred_element_type=jnp.float32
    )
    prediction = shift_sum(partial_value, ticks)
    resid = residual_of(prediction, measured, active)
    sent = jnp.stack([resid[:, :, k * share : k * share + span] for k in range(parts_y)], axis=0)
    got = lax.all_to_all(sent, "py", 0, 0)
    band_resid = jnp.transpose(got, (1, 0, 2, 3)).reshape(tile_x, width, span)
    stacked_band = gather_offsets(source, rows_wide, cols_all, tile_x, width)
    gradient = jnp.einsum(
        "oxysb,xysu->obu",
        stacked_band,
        windows(band_resid, share),
        preferred_element_type=jnp.float32,
    )
    summed = lax.psum(gradient, "px")
    return (prediction.astype(jnp.bfloat16), summed / 16)


def solution(mesh):
    in_specs = (
        P(),
        P("px", "py", None),
        P("px", "py", None),
        P("px", "py", None),
        P("px", "py"),
        P("px", "py", None),
        P(),
        P(),
    )
    out_specs = (P("px", "py", None), P(None, None, "py"))
    return jax.shard_map(
        on_device, mesh=mesh, in_specs=in_specs, out_specs=out_specs, check_vma=False
    )
```

profile of v0, /device:TPU:101, one launch (start us, length us, event | category | flops | bytes accessed | tf_op | source)
XLA Modules:
  0.0 386.6 jit_solution(15461394324954869272)
XLA Ops:
  7.2 0.7 convert_bitcast_fusion
  7.9 0.7 pad_maximum_fusion.1
  8.6 22.5 %all_gather.3 = f32[4,32,8,3]{2,0,3,1:T(4,128)S(1)} all-gather(f32[4,4,8,3]{2,0,3,1:T(4,128)S(1)} %copy.144), channel_id=1, replica_groups=mesh['px'=32,'py'=8] {'py'}, dimensions={1}, use_global_device_ids=true | all-gather | bytes 13824 | tf_op jit(solution)/shard_map/all_gather | solution.py:72
  31.2 8.9 %collective-permute-start.1 = (f32[2,32,8,3]{2,0,3,1:T(2,128)S(1)}, f32[2,32,8,3]{2,0,3,1:T(2,128)S(1)}, u32[]{:S(2)}, u32[]{:S(2)}) collective-permute-start(f32[2,32,8,3]{2,0,3,1:T(2,128)S(1)} %get-tuple-element.30), channel_id=1, source_target_pairs={{8,0},{16,8},{24,16},{32,24},{40,32},{48,40},{56,48},{64,56},{72,6... | collective-permute-start | bytes 18440 | tf_op jit(solution)/shard_map/ppermute | solution.py:13
  40.1 4.6 %collective-permute-start = (f32[2,32,8,3]{2,0,3,1:T(2,128)S(1)}, f32[2,32,8,3]{2,0,3,1:T(2,128)S(1)}, u32[]{:S(2)}, u32[]{:S(2)}) collective-permute-start(f32[2,32,8,3]{2,0,3,1:T(2,128)S(1)} %get-tuple-element.29), channel_id=1, source_target_pairs={{0,8},{8,16},{16,24},{24,32},{32,40},{40,48},{48,56},{56,64},{64,7... | collective-permute-start | bytes 18440 | tf_op jit(solution)/shard_map/ppermute | solution.py:13
  44.7 0.9 slice_compare_fusion
  45.6 0.7 pad_dynamic-slice_fusion.1
  46.4 0.7 pad_dynamic-slice_fusion
  47.4 0.7 convert_element_type.92
  48.7 2.9 convolution_convert_fusion
  54.3 1.3 slice-done
  55.6 0.6 slice-done.1
  56.1 2.6 fusion
  59.2 1.2 fusion.46
  62.0 0.3 bitcast_dynamic-update-slice_fusion.18
  62.6 0.3 bitcast_dynamic-update-slice_fusion.17
  63.0 0.3 bitcast_dynamic-update-slice_fusion.16
  63.3 0.3 bitcast_dynamic-update-slice_fusion.15
  63.7 0.3 bitcast_dynamic-update-slice_fusion.14
  64.3 0.3 bitcast_dynamic-update-slice_fusion.13
  64.7 0.3 bitcast_dynamic-update-slice_fusion.12
  65.0 0.3 bitcast_dynamic-update-slice_fusion.11
  65.8 0.3 bitcast_dynamic-update-slice_fusion.9
  66.5 0.3 bitcast_dynamic-update-slice_fusion.7
  66.9 0.3 bitcast_dynamic-update-slice_fusion.6
  67.5 0.3 bitcast_dynamic-update-slice_fusion.5
  67.9 0.3 bitcast_dynamic-update-slice_fusion.4
  68.2 0.5 bitcast_dynamic-update-slice_fusion.3
  68.7 0.3 bitcast_dynamic-update-slice_fusion.2
  69.5 2.0 multiply_convert_fusion
  71.5 4.6 %copy-done.1 = bf16[25,4,32,24,50]{4,3,2,1,0:T(8,128)(2,1)} copy-done((bf16[25,4,32,24,50]{4,3,2,1,0:T(8,128)(2,1)}, bf16[25,4,32,24,50]{4,3,2,1,0:T(8,128)(2,1)S(1)}, u32[]{:S(2)}) %copy-start.1) | copy-done | bytes 7680024
  76.1 0.6 constant_dynamic-update-slice_fusion.32
  76.7 0.7 constant_dynamic-update-slice_fusion.31
  77.3 0.7 constant_dynamic-update-slice_fusion.30
  78.0 0.7 constant_dynamic-update-slice_fusion.29
  78.7 0.7 constant_dynamic-update-slice_fusion.28
  79.4 0.7 constant_dynamic-update-slice_fusion.27
  80.0 0.7 constant_dynamic-update-slice_fusion.26
  80.7 0.7 constant_dynamic-update-slice_fusion.25
  81.4 5.4 %all-to-all-start = ((bf16[8,4,4,148]{3,2,1,0:T(4,128)(2,1)}), bf16[8,4,4,148]{3,2,1,0:T(4,128)(2,1)S(1)}, u32[]{:S(2)}, u32[]{:S(2)}) async-start(bf16[8,4,4,148]{3,2,1,0:T(4,128)(2,1)} %constant_dynamic-update-slice_fusion.25), calls=%async_computation | async-start | bytes 131072 | tf_op jit(solution)/shard_map/all_to_all | solution.py:94
  86.8 1.1 bitcast_dynamic-update-slice_fusion.1
  88.0 1.1 bitcast_dynamic-update-slice_fusion
  89.1 2.9 all-to-all-done
  92.1 0.4 slice_bitcast_fusion.1
  94.0 2.6 stack.359
  96.6 12.7 %convolution_bitcast_fusion = f32[25,50,125]{2,1,0:T(8,128)} fusion(bf16[25,4,32,24,50]{4,3,2,1,0:T(8,128)(2,1)} %bitcast_dynamic-update-slice_fusion, bf16[4,32,24,125]{3,2,1,0:T(8,128)(2,1)S(1)} %stack.359), kind=kOutput, calls=%fused_computation.6 | convolution fusion | flops 960000000 | bytes 9073000 | tf_op jit(solution)/shard_map/oxysb,xysu->obu/dot_general | solution.py:97
  109.3 268.5 %all-reduce.29.cloned.1.call-done = f32[25,50,125]{2,1,0:T(8,128)} async-done(((f32[25,50,125]{2,1,0:T(8,128)}), f32[25,50,125]{2,1,0:T(8,128)}) %all-reduce.29.cloned.1.call-update) | async-done | bytes 625016 | tf_op jit(solution)/shard_map/psum | solution.py:103
  377.8 2.0 broadcast_multiply_fusion
  (110 shorter events, 8.9 us)
Async XLA Ops:
  31.2 16.9 %collective-permute-start.1 = (f32[2,32,8,3]{2,0,3,1:T(2,128)S(1)}, f32[2,32,8,3]{2,0,3,1:T(2,128)S(1)}, u32[]{:S(2)}, u32[]{:S(2)}) collective-permute-start(f32[2,32,8,3]{2,0,3,1:T(2,128)S(1)} %get-tuple-element.30), channel_id=1, source_target_pairs={{8,0},{16,8},{24,16},{32,24},{40,32},{48,40},{56,48},{64,56},{72,6... | collective-permute-start | bytes 18440 | tf_op jit(solution)/shard_map/ppermute | solution.py:13
  40.1 8.2 %collective-permute-start = (f32[2,32,8,3]{2,0,3,1:T(2,128)S(1)}, f32[2,32,8,3]{2,0,3,1:T(2,128)S(1)}, u32[]{:S(2)}, u32[]{:S(2)}) collective-permute-start(f32[2,32,8,3]{2,0,3,1:T(2,128)S(1)} %get-tuple-element.29), channel_id=1, source_target_pairs={{0,8},{8,16},{16,24},{24,32},{32,40},{40,48},{48,56},{56,64},{64,7... | collective-permute-start | bytes 18440 | tf_op jit(solution)/shard_map/ppermute | solution.py:13
  53.4 2.2 slice-start
  53.7 2.4 slice-start.1
  68.7 0.8 copy-start
  69.4 6.7 %copy-start.1 = (bf16[25,4,32,24,50]{4,3,2,1,0:T(8,128)(2,1)}, bf16[25,4,32,24,50]{4,3,2,1,0:T(8,128)(2,1)S(1)}, u32[]{:S(2)}) copy-start(bf16[25,4,32,24,50]{4,3,2,1,0:T(8,128)(2,1)S(1)} %fusion.6) | copy-start | bytes 23040004
  81.4 10.6 %all-to-all-start = ((bf16[8,4,4,148]{3,2,1,0:T(4,128)(2,1)}), bf16[8,4,4,148]{3,2,1,0:T(4,128)(2,1)S(1)}, u32[]{:S(2)}, u32[]{:S(2)}) async-start(bf16[8,4,4,148]{3,2,1,0:T(4,128)(2,1)} %constant_dynamic-update-slice_fusion.25), calls=%async_computation | async-start | bytes 131072 | tf_op jit(solution)/shard_map/all_to_all | solution.py:94
  86.8 291.0 %all-reduce.29.cloned.1.call-start = ((), (), s32[]{:S(2)}) async-start(), calls=%async_computation.1 | async-start | bytes 1433600 | tf_op jit(solution)/shard_map/psum | solution.py:103
Sparse Core Ops, SparseCore 0:
  109.4 268.2 all-reduce.28
where the time goes:
time: 387 us
  waiting for transfers between devices  271 us (70%)
  blocking collectives  22.5 us (6%)
  local copies, waits for them, and re-layouts  21.4 us (6%)
  other arithmetic  19.5 us (5%)
  starting transfers between devices  18.9 us (5%)
  matrix products  18.2 us (5%)
  between operations  14.8 us (4%)
    psum x1, waiting for transfers between devices, on_device(): summed = lax.psum(gradient, 'px')  268 us
    all_gather x1, blocking collectives, on_device(): band = lax.all_gather(deposits, 'py', axis=1, tiled=True)  22.5 us
    ppermute x2, starting transfers between devices, passed_along(): return lax.ppermute(block, axis, route)  13.4 us
    dot_general x1, matrix products, on_device(): jnp.einsum('oxysb,xysu->obu', stacked_band, windows(band_resid, share), p...  12.7 us
    unnamed x41, local copies, waits for them, and re-layouts  12.4 us
    unnamed x47, other arithmetic  10.9 us
  transfers between devices with their start and end apart: 4, of which 2 were waited for; matrix products, arithmetic and copies ran while one was open for 2% of the time, Pallas kernels for 0%

commit v1 on v0

--- a/solution.py
+++ b/solution.py
@@ -69,7 +69,9 @@
     deposits = jnp.stack(
         [charge, hit_bins.astype(jnp.float32), hit_ticks.astype(jnp.float32)], axis=-1
     )
-    band = lax.all_gather(deposits, "py", axis=1, tiled=True)
+    band = jnp.concatenate(
+        lax.all_to_all(jnp.stack([deposits] * lax.axis_size("py")), "py", 0, 0), axis=1
+    )
     above = passed_along(band[tile_x - 2 :], "px", 1)
     below = passed_along(band[:2], "px", -1)
     wide = jnp.concatenate([above, band, below], axis=0)

time: 387 us -> 371 us (0.959)
  blocking collectives: 22.5 us -> 0 us
  waiting for transfers between devices: 271 us -> 277 us
    all_gather x1 -> x0, blocking collectives: 22.5 us -> none  [on_device(): band = lax.all_gather(deposits, 'py', axis=1, tiled=True)]
    all_to_all x0 -> x1, starting transfers between devices: none -> 4.82 us  [on_device(): lax.all_to_all(jnp.stack([deposits] * lax.axis_size('py')), 'py', 0, 0)]
    ppermute x2, starting transfers between devices: 13.4 us -> 9.18 us  [passed_along(): return lax.ppermute(block, axis, route)]
    unnamed x41 -> x44, local copies, waits for them, and re-layouts: 12.4 us -> 13.5 us
  transfers between devices with their start and end apart: 4 -> 5, of which waited for: 2 -> 4; matrix products, arithmetic and copies ran while one was open for 2% -> 2% of each run, Pallas kernels for 0% -> 0%
where the time goes in v1:
time: 371 us; the launch traced here: 370 us
  waiting for transfers between devices  277 us (75%)
  local copies, waits for them, and re-layouts  22.9 us (6%)
  other arithmetic  20.1 us (5%)
  matrix products  18.2 us (5%)
  starting transfers between devices  17.4 us (5%)
  between operations  14.8 us (4%)
    psum x1, waiting for transfers between devices, on_device(): summed = lax.psum(gradient, 'px')  271 us
    unnamed x44, local copies, waits for them, and re-layouts  13.5 us
    dot_general x1, matrix products, on_device(): jnp.einsum('oxysb,xysu->obu', stacked_band, windows(band_resid, share), p...  12.7 us
    unnamed x47, other arithmetic  10.9 us
    ppermute x2, starting transfers between devices, passed_along(): return lax.ppermute(block, axis, route)  9.18 us
  transfers between devices with their start and end apart: 5, of which 4 were waited for; matrix products, arithmetic and copies ran while one was open for 2% of the time, Pallas kernels for 0%

profile of v1, /device:TPU:101, one launch (start us, length us, event | category | flops | bytes accessed | tf_op | source)
XLA Modules:
  0.0 370.1 jit_solution(8022246002777217853)
XLA Ops:
  7.2 0.7 convert_bitcast_fusion
  7.9 0.7 pad_maximum_fusion.1
  8.6 0.8 reshape.925
  9.4 4.8 %all-to-all-start = ((f32[8,1,384]{2,1,0:T(1,128)}), f32[8,1,384]{2,1,0:T(1,128)S(1)}, u32[]{:S(2)}, u32[]{:S(2)}) async-start(f32[8,1,384]{2,1,0:T(1,128)} %reshape.925), calls=%async_computation | async-start | bytes 24576 | tf_op jit(solution)/shard_map/all_to_all | solution.py:73
  14.2 0.7 pad_dynamic-slice_fusion
  15.0 0.7 pad_dynamic-slice_fusion.1
  15.9 0.9 slice_compare_fusion
  16.8 2.5 all-to-all-done
  19.3 0.5 broadcast.904
  19.8 0.7 reduce
  20.8 4.0 %collective-permute-start.1 = (f32[2,32,8,3]{2,1,3,0:T(8,128)S(1)}, f32[2,32,8,3]{2,1,3,0:T(8,128)S(1)}, u32[]{:S(2)}, u32[]{:S(2)}) collective-permute-start(f32[2,32,8,3]{2,1,3,0:T(8,128)S(1)} %bitcast.410), channel_id=1, source_target_pairs={{8,0},{16,8},{24,16},{32,24},{40,32},{48,40},{56,48},{64,56},{72,6... | collective-permute-start | bytes 18440 | tf_op jit(solution)/shard_map/ppermute | solution.py:13
  24.9 5.2 %collective-permute-start = (f32[2,32,8,3]{2,1,3,0:T(8,128)S(1)}, f32[2,32,8,3]{2,1,3,0:T(8,128)S(1)}, u32[]{:S(2)}, u32[]{:S(2)}) collective-permute-start(f32[2,32,8,3]{2,1,3,0:T(8,128)S(1)} %bitcast.411), channel_id=1, source_target_pairs={{0,8},{8,16},{16,24},{24,32},{32,40},{40,48},{48,56},{56,64},{64,7... | collective-permute-start | bytes 18440 | tf_op jit(solution)/shard_map/ppermute | solution.py:13
  30.1 0.7 convert_element_type.92
  31.1 0.6 collective-permute-done
  32.1 2.9 convolution_convert_fusion
  37.7 1.3 slice-done
  39.0 0.6 slice-done.1
  39.5 2.6 fusion
  42.6 1.2 fusion.46
  45.4 0.3 bitcast_dynamic-update-slice_fusion.18
  46.0 0.3 bitcast_dynamic-update-slice_fusion.17
  46.4 0.3 bitcast_dynamic-update-slice_fusion.16
  47.1 0.3 bitcast_dynamic-update-slice_fusion.14
  47.7 0.3 bitcast_dynamic-update-slice_fusion.13
  48.1 0.3 bitcast_dynamic-update-slice_fusion.12
  50.3 0.3 bitcast_dynamic-update-slice_fusion.6
  50.9 0.3 bitcast_dynamic-update-slice_fusion.5
  51.6 0.5 bitcast_dynamic-update-slice_fusion.3
  52.1 0.3 bitcast_dynamic-update-slice_fusion.2
  52.9 2.0 multiply_convert_fusion
  54.9 4.5 %copy-done.1 = bf16[25,4,32,24,50]{4,3,2,1,0:T(8,128)(2,1)} copy-done((bf16[25,4,32,24,50]{4,3,2,1,0:T(8,128)(2,1)}, bf16[25,4,32,24,50]{4,3,2,1,0:T(8,128)(2,1)S(1)}, u32[]{:S(2)}) %copy-start.1) | copy-done | bytes 7680024
  59.4 0.6 constant_dynamic-update-slice_fusion.32
  60.0 0.7 constant_dynamic-update-slice_fusion.31
  60.7 0.7 constant_dynamic-update-slice_fusion.30
  61.4 0.7 constant_dynamic-update-slice_fusion.29
  62.0 0.7 constant_dynamic-update-slice_fusion.28
  62.7 0.7 constant_dynamic-update-slice_fusion.27
  63.4 0.7 constant_dynamic-update-slice_fusion.26
  64.1 0.7 constant_dynamic-update-slice_fusion.25
  64.7 3.4 all-to-all-start.1
  68.2 1.1 bitcast_dynamic-update-slice_fusion.1
  69.3 1.1 bitcast_dynamic-update-slice_fusion
  70.4 2.8 all-to-all-done.1
  73.4 0.4 slice_bitcast_fusion.1
  75.3 2.6 stack.371
  77.9 12.7 %convolution_bitcast_fusion = f32[25,50,125]{2,1,0:T(8,128)} fusion(bf16[25,4,32,24,50]{4,3,2,1,0:T(8,128)(2,1)} %bitcast_dynamic-update-slice_fusion, bf16[4,32,24,125]{3,2,1,0:T(8,128)(2,1)S(1)} %stack.371), kind=kOutput, calls=%fused_computation.6 | convolution fusion | flops 960000000 | bytes 9073000 | tf_op jit(solution)/shard_map/oxysb,xysu->obu/dot_general | solution.py:99
  90.6 270.7 %all-reduce.29.cloned.1.call-done = f32[25,50,125]{2,1,0:T(8,128)} async-done(((f32[25,50,125]{2,1,0:T(8,128)}), f32[25,50,125]{2,1,0:T(8,128)}) %all-reduce.29.cloned.1.call-update) | async-done | bytes 625016 | tf_op jit(solution)/shard_map/psum | solution.py:105
  361.3 2.0 broadcast_multiply_fusion
  (119 shorter events, 10.8 us)
Async XLA Ops:
  9.4 9.9 %all-to-all-start = ((f32[8,1,384]{2,1,0:T(1,128)}), f32[8,1,384]{2,1,0:T(1,128)S(1)}, u32[]{:S(2)}, u32[]{:S(2)}) async-start(f32[8,1,384]{2,1,0:T(1,128)} %reshape.925), calls=%async_computation | async-start | bytes 24576 | tf_op jit(solution)/shard_map/all_to_all | solution.py:73
  20.8 10.1 %collective-permute-start.1 = (f32[2,32,8,3]{2,1,3,0:T(8,128)S(1)}, f32[2,32,8,3]{2,1,3,0:T(8,128)S(1)}, u32[]{:S(2)}, u32[]{:S(2)}) collective-permute-start(f32[2,32,8,3]{2,1,3,0:T(8,128)S(1)} %bitcast.410), channel_id=1, source_target_pairs={{8,0},{16,8},{24,16},{32,24},{40,32},{48,40},{56,48},{64,56},{72,6... | collective-permute-start | bytes 18440 | tf_op jit(solution)/shard_map/ppermute | solution.py:13
  24.9 6.8 %collective-permute-start = (f32[2,32,8,3]{2,1,3,0:T(8,128)S(1)}, f32[2,32,8,3]{2,1,3,0:T(8,128)S(1)}, u32[]{:S(2)}, u32[]{:S(2)}) collective-permute-start(f32[2,32,8,3]{2,1,3,0:T(8,128)S(1)} %bitcast.411), channel_id=1, source_target_pairs={{0,8},{8,16},{16,24},{24,32},{32,40},{40,48},{48,56},{56,64},{64,7... | collective-permute-start | bytes 18440 | tf_op jit(solution)/shard_map/ppermute | solution.py:13
  36.8 2.2 slice-start
  37.1 2.4 slice-start.1
  52.1 0.8 copy-start
  52.8 6.7 %copy-start.1 = (bf16[25,4,32,24,50]{4,3,2,1,0:T(8,128)(2,1)}, bf16[25,4,32,24,50]{4,3,2,1,0:T(8,128)(2,1)S(1)}, u32[]{:S(2)}) copy-start(bf16[25,4,32,24,50]{4,3,2,1,0:T(8,128)(2,1)S(1)} %fusion.6) | copy-start | bytes 23040004
  64.7 8.5 %all-to-all-start.1 = ((bf16[8,4,4,148]{3,2,1,0:T(4,128)(2,1)}), bf16[8,4,4,148]{3,2,1,0:T(4,128)(2,1)S(1)}, u32[]{:S(2)}, u32[]{:S(2)}) async-start(bf16[8,4,4,148]{3,2,1,0:T(4,128)(2,1)} %constant_dynamic-update-slice_fusion.25), calls=%async_computation.1 | async-start | bytes 131072 | tf_op jit(solution)/shard_map/all_to_all | solution.py:96
  68.1 293.2 %all-reduce.29.cloned.1.call-start = ((), (), s32[]{:S(2)}) async-start(), calls=%async_computation.2 | async-start | bytes 1433600 | tf_op jit(solution)/shard_map/psum | solution.py:105
Sparse Core Ops, SparseCore 0:
  90.7 270.5 all-reduce.28
